TPU v7x, 256 devices: a whole 4x4x8 slice. The times are simulated.
256 devices in a mesh: rep: 2 (over y_hi), fsdp: 64 (over x, z, y_lo), tp: 2 (over core).
Axes of the slice: x: 4, y: 4 (y_hi: 2, y_lo: 2; y = y_hi * 2 + y_lo), z: 8, core: 2. Of those that a mesh axis runs over, the one named last changes fastest.
Arguments:
- attn_global: float32 [24, 1024, 1024], P('rep', 'fsdp', 'tp'), may hold values from -6 to 6
- attn_momentum: float32 [24, 1024, 1024], P('rep', 'fsdp', 'tp'), may hold values from -6 to 6
- attn_inner: bfloat16 [2, 24, 1024, 1024], P('rep', None, 'fsdp', 'tp'), may hold values from -6 to 6
- norm_global: float32 [4, 1024], P('rep', 'tp'), may hold values from 0.5 to 1.5
- norm_momentum: float32 [4, 1024], P('rep', 'tp'), may hold values from -4 to 4
- norm_inner: bfloat16 [2, 4, 1024], P('rep', None, 'tp'), may hold values from 0.5 to 1.5
- emb_global: float32 [64, 2, 251, 1024], P('fsdp', 'rep', None, 'tp'), may hold values from -6 to 6
- emb_momentum: float32 [64, 2, 251, 1024], P('fsdp', 'rep', None, 'tp'), may hold values from -6 to 6
- emb_inner: bfloat16 [2, 32128, 1024], P('rep', 'fsdp', 'tp'), may hold values from -6 to 6
- basis: float32 [1024, 64], replicated, may hold values from -0.1875 to 0.1875
- touched: int32 [2, 8192], replicated, may hold values from 0 to 32127
Outputs:
- new_attn_global: float32 [24, 1024, 1024], P('rep', 'fsdp', 'tp')
- new_attn_momentum: float32 [24, 1024, 1024], P('rep', 'fsdp', 'tp')
- attn_weights: float32 [24, 1024, 1024], P(None, 'fsdp', 'tp')
- new_norm_global: float32 [4, 1024], P('rep', 'tp')
- new_norm_momentum: float32 [4, 1024], P('rep', 'tp')
- norm_weights: float32 [4, 1024], P(None, 'tp')
- new_emb_global: float32 [64, 2, 251, 1024], P('fsdp', 'rep', None, 'tp')
- new_emb_momentum: float32 [64, 2, 251, 1024], P('fsdp', 'rep', None, 'tp')
- emb_weights: float32 [32128, 1024], P('fsdp', 'tp')
All inputs are finite; a program needn't handle non-finite values.
Results may differ from a plain program's by a relative error of at most 0.0003.
Values sent between devices are 32-bit elements; how exact they have to be, the bound alone decides.
No kernel may reach another device: no remote copies, remote signals or barrier semaphores. Data moves between devices by JAX's collectives and lax.ppermute only.
A program may use at most 64 MiB of HBM per device.

v0:
```python
import jax
import jax.numpy as jnp
from jax import lax
from jax.sharding import PartitionSpec as P

OUTER_RATE = 0.7
MOMENTUM = 0.9


def nesterov(global_part, momentum_part, outer_grad):
    fresh_momentum = MOMENTUM * momentum_part + outer_grad
    fresh_global = global_part - OUTER_RATE * (outer_grad + MOMENTUM * fresh_momentum)
    return (fresh_global, fresh_momentum)


def per_device(
    attn_global,
    attn_momentum,
    attn_inner,
    norm_global,
    norm_momentum,
    norm_inner,
    emb_global,
    emb_momentum,
    emb_inner,
    basis,
    touched,
):
    groups = lax.axis_size("rep") * 1.0
    rep_index = lax.axis_index("rep")
    attn_terms = attn_inner[0].astype(jnp.float32)
    norm_terms = norm_inner[0].astype(jnp.float32)
    attn_total, norm_total = lax.psum((attn_terms, norm_terms), "rep")
    attn_owned = attn_global.shape[0]
    norm_owned = norm_global.shape[0]
    attn_summed = lax.dynamic_slice_in_dim(attn_total, rep_index * attn_owned, attn_owned, 0)
    norm_summed = lax.dynamic_slice_in_dim(norm_total, rep_index * norm_owned, norm_owned, 0)
    new_attn_global, new_attn_momentum = nesterov(
        attn_global, attn_momentum, attn_global - attn_summed / groups
    )
    new_norm_global, new_norm_momentum = nesterov(
        norm_global, norm_momentum, norm_global - norm_summed / groups
    )
    block_rows = emb_inner.shape[1]
    half_rows = emb_global.shape[2]
    half_width = emb_global.shape[3]
    row_start = lax.axis_index("fsdp") * block_rows
    half_start = rep_index * half_rows
    positions = row_start + jnp.arange(block_rows, dtype=jnp.int32)
    matches = touched[:, :, None] == positions[None, None, :]
    touched_masks = jnp.any(matches, axis=1).astype(jnp.float32)
    counts = jnp.sum(touched_masks, axis=0)
    own_mask = lax.dynamic_index_in_dim(touched_masks, rep_index, 0, keepdims=False)
    half_counts = lax.dynamic_slice_in_dim(counts, half_start, half_rows, 0)
    basis_half = lax.dynamic_slice_in_dim(basis, lax.axis_index("tp") * half_width, half_width, 0)
    own_rows = emb_global[0, 0]
    own_momentum = emb_momentum[0, 0]
    global_coeff = jnp.dot(
        own_rows, basis_half, precision=lax.Precision.HIGHEST, preferred_element_type=jnp.float32
    )
    placed_global = lax.dynamic_update_slice_in_dim(
        jnp.zeros((block_rows, basis.shape[1]), jnp.float32),
        half_counts[:, None] * global_coeff,
        half_start,
        0,
    )
    inner_coeff = jnp.dot(
        emb_inner[0].astype(jnp.float32),
        basis_half,
        precision=lax.Precision.HIGHEST,
        preferred_element_type=jnp.float32,
    )
    coeff_term = placed_global - own_mask[:, None] * inner_coeff
    coeff_total = lax.psum(coeff_term.reshape(-1), ("rep", "tp")).reshape(coeff_term.shape)
    coeff_sum = lax.dynamic_slice_in_dim(coeff_total, half_start, half_rows, 0)
    emb_grad = (
        jnp.dot(
            coeff_sum,
            basis_half.T,
            precision=lax.Precision.HIGHEST,
            preferred_element_type=jnp.float32,
        )
        / groups
    )
    fresh_rows, fresh_momentum = nesterov(own_rows, own_momentum, emb_grad)
    new_emb_global = fresh_rows.reshape(emb_global.shape)
    new_emb_momentum = fresh_momentum.reshape(emb_momentum.shape)
    attn_weights, norm_weights, emb_halves = (
        lax.all_gather(new_attn_global, "rep", axis=0, tiled=True),
        lax.all_gather(new_norm_global, "rep", axis=0, tiled=True),
        lax.all_gather(new_emb_global, "rep", axis=1, tiled=True),
    )
    emb_weights = emb_halves.reshape(block_rows, half_width)
    return (
        new_attn_global,
        new_attn_momentum,
        attn_weights,
        new_norm_global,
        new_norm_momentum,
        norm_weights,
        new_emb_global,
        new_emb_momentum,
        emb_weights,
    )


def solution(mesh):
    placed = (
        P("rep", "fsdp", "tp"),
        P("rep", "fsdp", "tp"),
        P("rep", None, "fsdp", "tp"),
        P("rep", "tp"),
        P("rep", "tp"),
        P("rep", None, "tp"),
        P("fsdp", "rep", None, "tp"),
        P("fsdp", "rep", None, "tp"),
        P("rep", "fsdp", "tp"),
        P(),
        P(),
    )
    return jax.shard_map(
        per_device,
        mesh=mesh,
        in_specs=placed,
        out_specs=(
            P("rep", "fsdp", "tp"),
            P("rep", "fsdp", "tp"),
            P(None, "fsdp", "tp"),
            P("rep", "tp"),
            P("rep", "tp"),
            P(None, "tp"),
            P("fsdp", "rep", None, "tp"),
            P("fsdp", "rep", None, "tp"),
            P("fsdp", "tp"),
        ),
        check_vma=False,
    )
```

profile of v0, /device:TPU:2, one launch (start us, length us, event | category | flops | bytes accessed | tf_op | source)
XLA Modules:
  0.0 138.5 jit_solution(1538203716766188428)
XLA Ops:
  7.2 0.0 copy-start
  7.2 0.0 copy-start.3
  7.2 0.0 all-reduce.5.cloned.1.call-start
  7.3 5.2 %compare_reduce_fusion = pred[2,502]{1,0:T(4,128)(4,1)S(1)} fusion(s32[2,8192]{1,0:T(2,128)} %param.21, s32[502]{0:T(512)S(1)} %iota_add_fusion), kind=kLoop, calls=%fused_computation | loop fusion | flops 16448532 | bytes 68548 | tf_op jit(solution)/shard_map/reduce_or | solution.py:51
  12.5 0.0 copy-start.5
  12.5 0.1 dynamic_slice.21
  12.6 1.7 %fusion.2 = f32[251,64]{0,1:T(8,128)S(1)} fusion(f32[1,1,251,512]{3,1,2,0:T(1,128)} %param.17, f32[1024,64]{0,1:T(8,128)} %param.20, s32[]{:T(128)S(6)} %select_n.21, f32[251]{0:T(256)S(1)} %dynamic_slice.21), kind=kOutput, calls=%fused_computation.6 | convolution fusion | flops 98713280 | bytes 710384 | tf_op jit(solution)/shard_map/dot_general | solution.py:58
  14.3 0.7 dynamic_update_slice.3
  15.0 1.3 fusion.1
  16.3 0.0 all-reduce.5.cloned.1.call-update
  16.3 0.0 copy-start.1
  16.3 0.0 copy-start.4
  16.3 0.0 all-reduce.3.cloned.1.call-start
  16.4 1.0 bitcast_convert_fusion
  17.4 0.0 all-reduce.3.cloned.1.call-update
  17.4 0.0 copy-done.9
  17.4 6.5 %psum.22 = f32[4,512]{1,0:T(4,128)S(1)} all-reduce(f32[4,512]{1,0:T(4,128)S(1)} %bitcast_convert_fusion.1), channel_id=1, replica_groups=mesh['rep'=2,'fsdp'=64,'tp'=2] {'rep'}, use_global_device_ids=true, to_apply=%region_1.0 | all-reduce | flops 2048 | bytes 16384 | tf_op jit(solution)/shard_map/psum | solution.py:33
  23.9 0.0 copy-done.10
  23.9 0.6 multiply_subtract_fusion.2
  24.6 5.9 %all-gather.1 = f32[2,2,512]{2,1,0:T(2,128)S(1)} all-gather(f32[1,2,512]{2,1,0:T(2,128)S(1)} %bitcast.41), channel_id=1, replica_groups=mesh['rep'=2,'fsdp'=64,'tp'=2] {'rep'}, dimensions={0}, use_global_device_ids=true | all-gather | bytes 12288 | tf_op jit(solution)/shard_map/all_gather | solution.py:90
  30.4 0.6 reshape.58
  31.0 33.8 %all-reduce.5.cloned.1.call-done = f32[502,64]{0,1:T(8,128)} async-done(((f32[502,64]{0,1:T(8,128)}), f32[502,64]{0,1:T(8,128)}) %all-reduce.5.cloned.1.call-update) | async-done | bytes 128528 | tf_op jit(solution)/shard_map/psum | solution.py:74
  64.8 1.7 %fusion.14 = (f32[1,251,512]{2,1,0:T(8,128)S(1)}, f32[1,1,251,512]{3,2,1,0:T(8,128)S(1)}, f32[1,1,251,512]{3,2,1,0:T(8,128)S(1)}) fusion(f32[1,1,251,512]{3,1,2,0:T(1,128)S(1)} %copy-done.4, f32[1,1,251,512]{3,1,2,0:T(1,128)S(1)} %copy-done.1, f32[1024,64]{0,1:T(8,128)S(1)} %copy-done.3, s32[]{:T(128)S(6)} %select_n.21, ...), kind=kOutput, calls=%fused_computation.32 | convolution fusion | flops 99596800 | bytes 2766856 | tf_op jit(solution)/shard_map/dot_general | solution.py:77
  66.6 0.0 copy-done.8
  66.6 17.8 %all-gather.2 = f32[2,251,512]{2,1,0:T(8,128)S(1)} all-gather(f32[1,251,512]{2,1,0:T(8,128)S(1)} %get-tuple-element.49), channel_id=2, replica_groups=mesh['rep'=2,'fsdp'=64,'tp'=2] {'rep'}, dimensions={0}, use_global_device_ids=true | all-gather | bytes 1542144 | tf_op jit(solution)/shard_map/all_gather | solution.py:91
  84.4 1.1 reshape.60
  85.5 1.3 copy.30
  86.8 1.3 copy.31
  88.1 27.9 %all-reduce.3.cloned.1.call-done = f32[24,16,512]{2,1,0:T(8,128)} async-done(((f32[24,16,512]{2,1,0:T(8,128)}), f32[24,16,512]{2,1,0:T(8,128)}) %all-reduce.3.cloned.1.call-update) | async-done | bytes 786448 | tf_op jit(solution)/shard_map/psum | solution.py:33
  116.0 1.9 %multiply_subtract_fusion = (f32[12,16,512]{2,1,0:T(8,128)S(1)}, f32[12,16,512]{2,1,0:T(8,128)}) fusion(f32[12,16,512]{2,1,0:T(8,128)S(1)} %copy-done.6, f32[24,16,512]{2,1,0:T(8,128)} %all-reduce.3.cloned.1.call-done, s32[]{:T(128)S(6)} %select_n.18, f32[12,16,512]{2,1,0:T(8,128)S(1)} %copy-done.7), kind=kLoop, calls=%fused_computation.14 | loop fusion | flops 786432 | bytes 1966084 | tf_op jit(solution)/shard_map/sub | solution.py:12
  117.9 12.8 %all_gather.9 = f32[24,16,512]{2,1,0:T(8,128)S(1)} all-gather(f32[12,16,512]{2,1,0:T(8,128)S(1)} %get-tuple-element.61), channel_id=1, replica_groups=mesh['rep'=2,'fsdp'=64,'tp'=2] {'rep'}, dimensions={0}, use_global_device_ids=true | all-gather | bytes 1179648 | tf_op jit(solution)/shard_map/all_gather | solution.py:89
  130.8 0.9 copy.57
  (22 shorter events, 0.1 us)
Async XLA Ops:
  7.2 7.8 %copy-start = (bf16[1,502,512]{2,1,0:T(8,128)(2,1)S(1)}, bf16[1,502,512]{2,1,0:T(8,128)(2,1)}, u32[]{:S(2)}) copy-start(bf16[1,502,512]{2,1,0:T(8,128)(2,1)} %param.19) | copy-start | bytes 1542148
  7.2 7.8 %copy-start.3 = (f32[1024,64]{0,1:T(8,128)S(1)}, f32[1024,64]{0,1:T(8,128)}, u32[]{:S(2)}) copy-start(f32[1024,64]{0,1:T(8,128)} %param.20) | copy-start | bytes 786436
  7.2 57.6 %all-reduce.5.cloned.1.call-start = ((), (), s32[]{:S(2)}) async-start(), calls=%async_computation.1 | async-start | bytes 262144 | tf_op jit(solution)/shard_map/psum | solution.py:74
  12.5 3.9 %copy-start.5 = (bf16[1,24,16,512]{3,2,1,0:T(8,128)(2,1)S(1)}, bf16[1,24,16,512]{3,2,1,0:T(8,128)(2,1)}, u32[]{:S(2)}) copy-start(bf16[1,24,16,512]{3,2,1,0:T(8,128)(2,1)} %param.13) | copy-start | bytes 1179652
  16.3 1.1 copy-start.9
  16.3 7.6 %copy-start.10 = (f32[2,512]{1,0:T(2,128)S(1)}, f32[2,512]{1,0:T(2,128)}, u32[]{:S(2)}) copy-start(f32[2,512]{1,0:T(2,128)} %param.14) | copy-start | bytes 12292
  16.3 7.6 %copy-start.11 = (f32[2,512]{1,0:T(2,128)S(1)}, f32[2,512]{1,0:T(2,128)}, u32[]{:S(2)}) copy-start(f32[2,512]{1,0:T(2,128)} %param.15) | copy-start | bytes 12292
  16.3 48.5 %copy-start.1 = (f32[1,1,251,512]{3,1,2,0:T(1,128)S(1)}, f32[1,1,251,512]{3,1,2,0:T(1,128)}, u32[]{:S(2)}) copy-start(f32[1,1,251,512]{3,1,2,0:T(1,128)} %param.17) | copy-start | bytes 1542148
  16.3 48.5 %copy-start.4 = (f32[1,1,251,512]{3,1,2,0:T(1,128)S(1)}, f32[1,1,251,512]{3,1,2,0:T(1,128)}, u32[]{:S(2)}) copy-start(f32[1,1,251,512]{3,1,2,0:T(1,128)} %param.18) | copy-start | bytes 1542148
  16.3 99.7 %all-reduce.3.cloned.1.call-start = ((), (), s32[]{:S(2)}) async-start(), calls=%async_computation | async-start | bytes 1572864 | tf_op jit(solution)/shard_map/psum | solution.py:33
  24.6 42.0 %copy-start.8 = (f32[2,512]{1,0:T(2,128)}, f32[2,512]{1,0:T(2,128)S(1)}, u32[]{:S(2)}) copy-start(f32[2,512]{1,0:T(2,128)S(1)} %get-tuple-element.64) | copy-start | bytes 12292
  85.5 30.6 %copy-start.6 = (f32[12,16,512]{2,1,0:T(8,128)S(1)}, f32[12,16,512]{2,1,0:T(8,128)}, u32[]{:S(2)}) copy-start(f32[12,16,512]{2,1,0:T(8,128)} %param.11) | copy-start | bytes 1179652
  85.5 30.6 %copy-start.7 = (f32[12,16,512]{2,1,0:T(8,128)S(1)}, f32[12,16,512]{2,1,0:T(8,128)}, u32[]{:S(2)}) copy-start(f32[12,16,512]{2,1,0:T(8,128)} %param.12) | copy-start | bytes 1179652
  117.9 13.7 %copy-start.2 = (f32[12,16,512]{2,1,0:T(8,128)}, f32[12,16,512]{2,1,0:T(8,128)S(1)}, u32[]{:S(2)}) copy-start(f32[12,16,512]{2,1,0:T(8,128)S(1)} %get-tuple-element.61) | copy-start | bytes 1179652
Sparse Core Ops, SparseCore 0:
  16.4 48.3 all-reduce.4
  68.0 47.9 all-reduce.2
where the time goes:
time: 139 us; the launch traced here: 138 us
  waiting for transfers between devices  61.8 us (44%)
  blocking collectives  43 us (31%)
  between operations  14.2 us (10%)
  other arithmetic  8.68 us (6%)
  local copies, waits for them, and re-layouts  6 us (4%)
  matrix products  4.69 us (3%)
    psum x1, waiting for transfers between devices, per_device(): lax.psum(coeff_term.reshape(-1), ('rep', 'tp')).reshape(coeff_term.shape)  33.8 us
    psum x1, waiting for transfers between devices, per_device(): attn_total, norm_total = lax.psum((attn_terms, norm_terms), 'rep')  27.9 us
    all_gather x1, blocking collectives, per_device(): lax.all_gather(new_emb_global, 'rep', axis=1, tiled=True)  17.8 us
    all_gather x1, blocking collectives, per_device(): lax.all_gather(new_attn_global, 'rep', axis=0, tiled=True)  12.8 us
    psum x1, blocking collectives, per_device(): attn_total, norm_total = lax.psum((attn_terms, norm_terms), 'rep')  6.51 us
    all_gather x1, blocking collectives, per_device(): lax.all_gather(new_norm_global, 'rep', axis=0, tiled=True)  5.85 us
    unnamed x29, local copies, waits for them, and re-layouts  5.24 us
    reduce_or x1, other arithmetic, per_device(): touched_masks = jnp.any(matches, axis=1).astype(jnp.float32)  5.18 us
  transfers between devices with their start and end apart: 2, of which 2 were waited for; matrix products, arithmetic and copies ran while one was open for 5% of the time, Pallas kernels for 0%

commit v1 on v0

--- a/solution.py
+++ b/solution.py
@@ -5,6 +5,11 @@
 
 OUTER_RATE = 0.7
 MOMENTUM = 0.9
+
+
+def add_all(x, axis):
+    parts = lax.all_gather(x, axis)
+    return jnp.sum(parts, axis=0)
 
 
 def nesterov(global_part, momentum_part, outer_grad):
@@ -71,7 +76,7 @@
         preferred_element_type=jnp.float32,
     )
     coeff_term = placed_global - own_mask[:, None] * inner_coeff
-    coeff_total = lax.psum(coeff_term.reshape(-1), ("rep", "tp")).reshape(coeff_term.shape)
+    coeff_total = add_all(coeff_term.reshape(-1), ("rep", "tp")).reshape(coeff_term.shape)
     coeff_sum = lax.dynamic_slice_in_dim(coeff_total, half_start, half_rows, 0)
     emb_grad = (
         jnp.dot(

time: 139 us -> 87.5 us (0.63)
  waiting for transfers between devices: 61.8 us -> 0.02 us
  blocking collectives: 43 us -> 54.3 us
  matrix products: 4.69 us -> 2.94 us
    psum x1 -> x0, waiting for transfers between devices: 33.8 us -> none  [per_device(): lax.psum(coeff_term.reshape(-1), ('rep', 'tp')).reshape(coeff_term.shape)]
    psum x1, waiting for transfers between devices: 27.9 us -> 0.01 us  [per_device(): attn_total, norm_total = lax.psum((attn_terms, norm_terms), 'rep')]
    all_gather x0 -> x1, blocking collectives: none -> 8.89 us  [add_all(): parts = lax.all_gather(x, axis)]
    all_gather x1, blocking collectives: 17.8 us -> 21.1 us  [per_device(): lax.all_gather(new_emb_global, 'rep', axis=1, tiled=True)]
    unnamed x29 -> x28, local copies, waits for them, and re-layouts: 5.24 us -> 5.42 us
  transfers between devices with their start and end apart: 2 -> 1, of which waited for: 2 -> 0; matrix products, arithmetic and copies ran while one was open for 5% -> 16% of each run, Pallas kernels for 0% -> 0%
where the time goes in v1:
time: 87.5 us; the launch traced here: 87.3 us
  blocking collectives  54.3 us (62%)
  between operations  14.2 us (16%)
  other arithmetic  9.36 us (11%)
  local copies, waits for them, and re-layouts  6.4 us (7%)
  matrix products  2.94 us (3%)
    all_gather x1, blocking collectives, per_device(): lax.all_gather(new_emb_global, 'rep', axis=1, tiled=True)  21.1 us
    all_gather x1, blocking collectives, per_device(): lax.all_gather(new_attn_global, 'rep', axis=0, tiled=True)  11.7 us
    all_gather x1, blocking collectives, add_all(): parts = lax.all_gather(x, axis)  8.89 us
    psum x1, blocking collectives, per_device(): attn_total, norm_total = lax.psum((attn_terms, norm_terms), 'rep')  6.79 us
    all_gather x1, blocking collectives, per_device(): lax.all_gather(new_norm_global, 'rep', axis=0, tiled=True)  5.85 us
    unnamed x28, local copies, waits for them, and re-layouts  5.42 us
    reduce_or x1, other arithmetic, per_device(): touched_masks = jnp.any(matches, axis=1).astype(jnp.float32)  4.29 us
    sub x2, other arithmetic, nesterov(): global_part - OUTER_RATE * (outer_grad + MOMENTUM * fresh_momentum)  2.49 us
  transfers between devices with their start and end apart: 1, of which 0 were waited for; matrix products, arithmetic and copies ran while one was open for 16% of the time, Pallas kernels for 0%

profile of v1, /device:TPU:2, one launch (start us, length us, event | category | flops | bytes accessed | tf_op | source)
XLA Modules:
  0.0 87.3 jit_solution(2578945215081955666)
XLA Ops:
  7.2 0.0 copy-start
  7.2 0.0 copy-start.6
  7.2 0.0 copy-start.1
  7.2 0.0 all-reduce.2.cloned.1.call-start
  7.3 2.1 %bitcast_convert_fusion = f32[24,16,512]{2,1,0:T(8,128)} fusion(bf16[1,24,16,512]{3,2,1,0:T(8,128)(2,1)} %param.13), kind=kLoop, calls=%fused_computation.13 | loop fusion | flops 196608 | bytes 1179648 | tf_op jit(solution)/shard_map/convert_element_type | solution.py:36
  9.3 0.0 all-reduce.2.cloned.1.call-update
  9.4 4.3 %compare_reduce_fusion = pred[2,502]{1,0:T(4,128)(4,1)S(1)} fusion(s32[2,8192]{1,0:T(2,128)S(1)} %copy-done.6, s32[502]{0:T(512)S(1)} %iota_add_fusion), kind=kLoop, calls=%fused_computation | loop fusion | flops 16448532 | bytes 68548 | tf_op jit(solution)/shard_map/reduce_or | solution.py:56
  13.7 0.1 dynamic_slice.21
  13.8 0.0 copy-done.3
  13.8 0.6 fusion.2
  14.4 0.7 dynamic_update_slice.3
  15.1 0.6 fusion.1
  15.7 0.1 copy.31
  15.9 0.2 reshape.54
  16.1 8.9 %all-gather.2 = f32[4,1,32128]{2,1,0:T(1,128)S(1)} all-gather(f32[1,1,32128]{2,1,0:T(1,128)S(1)} %reshape.54), channel_id=1, replica_groups=mesh['rep'=2,'fsdp'=64,'tp'=2] {'rep','tp'}, dimensions={0}, use_global_device_ids=true | all-gather | bytes 642560 | tf_op jit(solution)/shard_map/all_gather | solution.py:11
  24.9 0.5 reduce_sum.19
  25.4 0.1 reshape.44
  25.5 1.7 %fusion.14 = (f32[1,251,512]{2,1,0:T(8,128)S(1)}, f32[1,1,251,512]{3,2,1,0:T(8,128)S(1)}, f32[1,1,251,512]{3,2,1,0:T(8,128)S(1)}) fusion(f32[1,1,251,512]{3,1,2,0:T(1,128)} %param.18, f32[1,1,251,512]{3,1,2,0:T(1,128)S(1)} %copy-done.1, f32[1024,64]{0,1:T(8,128)S(1)} %copy-done.3, s32[]{:T(128)S(6)} %select_n.21, f32[502,64]{1,0:T(8,128)S(1)} %reshape.44, ...), kind=kOutput, calls=%fused_computation.32 | convolution fusion | flops 99596800 | bytes 2832392 | tf_op jit(solution)/shard_map/dot_general | solution.py:82
  27.3 21.1 %all-gather.3 = f32[2,251,512]{2,1,0:T(8,128)S(1)} all-gather(f32[1,251,512]{2,1,0:T(8,128)S(1)} %get-tuple-element.49), channel_id=2, replica_groups=mesh['rep'=2,'fsdp'=64,'tp'=2] {'rep'}, dimensions={0}, use_global_device_ids=true | all-gather | bytes 1542144 | tf_op jit(solution)/shard_map/all_gather | solution.py:96
  48.4 1.1 %reshape.57 = f32[502,512]{1,0:T(8,128)} reshape(f32[2,251,512]{2,1,0:T(8,128)S(1)} %all-gather.3) | data formatting | bytes 2056192
  49.4 0.0 copy-start.5
  49.5 1.3 %copy.33 = f32[1,1,251,512]{3,1,2,0:T(1,128)} copy(f32[1,1,251,512]{3,2,1,0:T(8,128)S(1)} %get-tuple-element.50) | data formatting | bytes 1028096
  50.8 1.3 %copy.34 = f32[1,1,251,512]{3,1,2,0:T(1,128)} copy(f32[1,1,251,512]{3,2,1,0:T(8,128)S(1)} %get-tuple-element.51) | data formatting | bytes 1028096
  52.1 6.8 %psum.15 = f32[4,512]{1,0:T(4,128)S(1)} all-reduce(f32[4,512]{1,0:T(4,128)S(1)} %bitcast_convert_fusion.1), channel_id=1, replica_groups=mesh['rep'=2,'fsdp'=64,'tp'=2] {'rep'}, use_global_device_ids=true, to_apply=%region_1.0 | all-reduce | flops 2048 | bytes 16384 | tf_op jit(solution)/shard_map/psum | solution.py:38
  58.9 0.0 copy-done.9
  58.9 0.6 multiply_subtract_fusion.2
  59.5 5.9 %all-gather.1 = f32[2,2,512]{2,1,0:T(2,128)S(1)} all-gather(f32[1,2,512]{2,1,0:T(2,128)S(1)} %bitcast.41), channel_id=1, replica_groups=mesh['rep'=2,'fsdp'=64,'tp'=2] {'rep'}, dimensions={0}, use_global_device_ids=true | all-gather | bytes 12288 | tf_op jit(solution)/shard_map/all_gather | solution.py:95
  65.4 0.6 reshape.53
  66.0 0.0 copy-done.4
  66.0 1.9 %multiply_subtract_fusion = (f32[12,16,512]{2,1,0:T(8,128)S(1)}, f32[12,16,512]{2,1,0:T(8,128)}) fusion(f32[12,16,512]{2,1,0:T(8,128)S(1)} %copy-done.4, f32[24,16,512]{2,1,0:T(8,128)} %all-reduce.2.cloned.1.call-done, s32[]{:T(128)S(6)} %select_n.18, f32[12,16,512]{2,1,0:T(8,128)S(1)} %copy-done.5), kind=kLoop, calls=%fused_computation.14 | loop fusion | flops 786432 | bytes 1966084 | tf_op jit(solution)/shard_map/sub | solution.py:17
  67.9 11.7 %all_gather.12 = f32[24,16,512]{2,1,0:T(8,128)S(1)} all-gather(f32[12,16,512]{2,1,0:T(8,128)S(1)} %get-tuple-element.61), channel_id=1, replica_groups=mesh['rep'=2,'fsdp'=64,'tp'=2] {'rep'}, dimensions={0}, use_global_device_ids=true | all-gather | bytes 1179648 | tf_op jit(solution)/shard_map/all_gather | solution.py:94
  79.5 0.9 %copy.59 = f32[24,16,512]{2,1,0:T(8,128)} copy(f32[24,16,512]{2,1,0:T(8,128)S(1)} %all_gather.12) | data formatting | bytes 1572864
  (22 shorter events, 0.1 us)
Async XLA Ops:
  7.2 7.9 %copy-start = (bf16[1,502,512]{2,1,0:T(8,128)(2,1)S(1)}, bf16[1,502,512]{2,1,0:T(8,128)(2,1)}, u32[]{:S(2)}) copy-start(bf16[1,502,512]{2,1,0:T(8,128)(2,1)} %param.19) | copy-start | bytes 1542148
  7.2 2.2 %copy-start.6 = (s32[2,8192]{1,0:T(2,128)S(1)}, s32[2,8192]{1,0:T(2,128)}, u32[]{:S(2)}) copy-start(s32[2,8192]{1,0:T(2,128)} %param.21) | copy-start | bytes 196612
  7.2 6.6 %copy-start.1 = (f32[1,1,251,512]{3,1,2,0:T(1,128)S(1)}, f32[1,1,251,512]{3,1,2,0:T(1,128)}, u32[]{:S(2)}) copy-start(f32[1,1,251,512]{3,1,2,0:T(1,128)} %param.17) | copy-start | bytes 1542148
  7.2 6.6 %copy-start.3 = (f32[1024,64]{0,1:T(8,128)S(1)}, f32[1024,64]{0,1:T(8,128)}, u32[]{:S(2)}) copy-start(f32[1024,64]{0,1:T(8,128)} %param.20) | copy-start | bytes 786436
  7.2 58.8 %all-reduce.2.cloned.1.call-start = ((), (), s32[]{:S(2)}) async-start(), calls=%async_computation | async-start | bytes 1572864 | tf_op jit(solution)/shard_map/psum | solution.py:38
  49.4 2.7 %copy-start.8 = (bf16[1,4,512]{2,1,0:T(4,128)(2,1)S(1)}, bf16[1,4,512]{2,1,0:T(4,128)(2,1)}, u32[]{:S(2)}) copy-start(bf16[1,4,512]{2,1,0:T(4,128)(2,1)} %param.16) | copy-start | bytes 12292
  49.4 9.4 %copy-start.9 = (f32[2,512]{1,0:T(2,128)S(1)}, f32[2,512]{1,0:T(2,128)}, u32[]{:S(2)}) copy-start(f32[2,512]{1,0:T(2,128)} %param.14) | copy-start | bytes 12292
  49.4 9.4 %copy-start.10 = (f32[2,512]{1,0:T(2,128)S(1)}, f32[2,512]{1,0:T(2,128)}, u32[]{:S(2)}) copy-start(f32[2,512]{1,0:T(2,128)} %param.15) | copy-start | bytes 12292
  49.4 16.5 %copy-start.4 = (f32[12,16,512]{2,1,0:T(8,128)S(1)}, f32[12,16,512]{2,1,0:T(8,128)}, u32[]{:S(2)}) copy-start(f32[12,16,512]{2,1,0:T(8,128)} %param.11) | copy-start | bytes 1179652
  49.4 16.5 %copy-start.5 = (f32[12,16,512]{2,1,0:T(8,128)S(1)}, f32[12,16,512]{2,1,0:T(8,128)}, u32[]{:S(2)}) copy-start(f32[12,16,512]{2,1,0:T(8,128)} %param.12) | copy-start | bytes 1179652
  59.5 20.0 %copy-start.7 = (f32[2,512]{1,0:T(2,128)}, f32[2,512]{1,0:T(2,128)S(1)}, u32[]{:S(2)}) copy-start(f32[2,512]{1,0:T(2,128)S(1)} %get-tuple-element.64) | copy-start | bytes 12292
  67.9 12.6 %copy-start.2 = (f32[12,16,512]{2,1,0:T(8,128)}, f32[12,16,512]{2,1,0:T(8,128)S(1)}, u32[]{:S(2)}) copy-start(f32[12,16,512]{2,1,0:T(8,128)S(1)} %get-tuple-element.61) | copy-start | bytes 1179652
Sparse Core Ops, SparseCore 0:
  11.2 53.4 all-reduce.1
